TPU v7x, 256 devices: a whole 4x4x8 slice. The times are simulated.
256 devices in a mesh: dp: 32 (over x, z_hi, y), mp: 8 (over z_lo, core).
Axes of the slice: x: 4, y: 4, z: 8 (z_hi: 2, z_lo: 4; z = z_hi * 4 + z_lo), core: 2. Of those that a mesh axis runs over, the one named last changes fastest.
Arguments:
- forget_rows: bfloat16 [1024, 8192], P('dp', 'mp'), may hold values from -6 to 6
- cotangent: bfloat16 [1024, 8192], P('dp', 'mp'), may hold values from -6 to 6
- retain_rows: bfloat16 [1024, 8192], P('dp', 'mp'), may hold values from -6 to 6
- w_gate: bfloat16 [8192, 16384], P('mp', 'dp'), may hold values from -5 to 5
- w_up: bfloat16 [8192, 16384], P('mp', 'dp'), may hold values from -5 to 5
- w_down: bfloat16 [16384, 8192], P('dp', 'mp'), may hold values from -5 to 5
Outputs:
- retained: bfloat16 [1024, 8192], P('dp', 'mp')
- new_gate: bfloat16 [8192, 16384], P('mp', 'dp')
- new_up: bfloat16 [8192, 16384], P('mp', 'dp')
- new_down: bfloat16 [16384, 8192], P('dp', 'mp')
All inputs are finite; a program needn't handle non-finite values.
Results may differ from a plain program's by a relative error of at most 0.0071.
Values may be sent and summed in bfloat16 or wider, within the bound.
No kernel may reach another device: no remote copies, remote signals or barrier semaphores. Data moves between devices by JAX's collectives and lax.ppermute only.
A program may use at most 64 MiB of HBM per device.

v0:
```python
import math
import jax
import jax.numpy as jnp
from jax import lax
from jax.sharding import PartitionSpec as P

D = 8192
FF = 16384
STEP_SIZE = 0.5


def project_sum(rows_all, weight_pair):
    width_scale = 1.0 / math.sqrt(D)
    return lax.psum_scatter(
        jnp.dot(rows_all, weight_pair, preferred_element_type=jnp.float32) * width_scale,
        "mp",
        scatter_dimension=0,
        tiled=True,
    )


def gather_units(values):
    return lax.all_gather(values, "mp", axis=0, tiled=True)


def activate(sums, unit_count):
    gate_sum = sums[:, :unit_count]
    up_sum = sums[:, unit_count:]
    sigmoid_gate = jax.nn.sigmoid(gate_sum)
    return (gate_sum, up_sum, sigmoid_gate, gate_sum * sigmoid_gate)


def unit_grads(back_units, gate_sum, up_sum, sigmoid_gate, active):
    grad_gate = back_units * up_sum * sigmoid_gate * (1.0 + gate_sum * (1.0 - sigmoid_gate))
    grad_up = back_units * active
    return jnp.concatenate([grad_gate, grad_up], axis=1).astype(jnp.bfloat16)


def body(forget_rows, cotangent, retain_rows, w_gate, w_up, w_down):
    unit_count = w_gate.shape[1]
    width_scale = 1.0 / math.sqrt(D)
    contract_rows = (((0,), (0,)), ((), ()))
    contract_cols = (((1,), (1,)), ((), ()))
    forget_all, cotan_all, retain_all = (
        lax.all_gather(forget_rows, "dp", axis=0, tiled=True),
        lax.all_gather(cotangent, "dp", axis=0, tiled=True),
        lax.all_gather(retain_rows, "dp", axis=0, tiled=True),
    )
    total_rows = forget_all.shape[0]
    token_scale = 1.0 / math.sqrt(total_rows)
    weight_pair = jnp.concatenate([w_gate, w_up], axis=1)
    sums = project_sum(forget_all, weight_pair)
    gate_sum, up_sum, sigmoid_gate, active = activate(sums, unit_count)
    hidden = (active * up_sum).astype(jnp.bfloat16)
    hidden_all = gather_units(hidden)
    block_rows = cotan_all
    back_units = lax.psum_scatter(
        lax.dot_general(block_rows, w_down, contract_cols, preferred_element_type=jnp.float32)
        * width_scale,
        "mp",
        scatter_dimension=0,
        tiled=True,
    )
    grads_all = gather_units(unit_grads(back_units, gate_sum, up_sum, sigmoid_gate, active))
    grad_down = (
        lax.dot_general(hidden_all, cotan_all, contract_rows, preferred_element_type=jnp.float32)
        * token_scale
    )
    grad_pair = (
        lax.dot_general(forget_all, grads_all, contract_rows, preferred_element_type=jnp.float32)
        * token_scale
    )
    new_gate = (w_gate.astype(jnp.float32) + STEP_SIZE * grad_pair[:, :unit_count]).astype(
        jnp.bfloat16
    )
    new_up = (w_up.astype(jnp.float32) + STEP_SIZE * grad_pair[:, unit_count:]).astype(jnp.bfloat16)
    new_down = (w_down.astype(jnp.float32) + STEP_SIZE * grad_down).astype(jnp.bfloat16)
    new_pair = jnp.concatenate([new_gate, new_up], axis=1)
    keep_sums = project_sum(retain_all, new_pair)
    gate_keep, up_keep, sigmoid_keep, active_keep = activate(keep_sums, unit_count)
    hidden_keep = (active_keep * up_keep).astype(jnp.bfloat16)
    hidden_keep_all = gather_units(hidden_keep)
    out_scale = 1.0 / math.sqrt(FF)
    block_rows = hidden_keep_all
    retained = lax.psum_scatter(
        jnp.dot(block_rows, new_down, preferred_element_type=jnp.float32) * out_scale,
        "dp",
        scatter_dimension=0,
        tiled=True,
    ).astype(jnp.bfloat16)
    return (retained, new_gate, new_up, new_down)


def solution(mesh):
    in_specs = (
        P("dp", "mp"),
        P("dp", "mp"),
        P("dp", "mp"),
        P("mp", "dp"),
        P("mp", "dp"),
        P("dp", "mp"),
    )
    out_specs = (P("dp", "mp"), P("mp", "dp"), P("mp", "dp"), P("dp", "mp"))
    return jax.shard_map(body, mesh=mesh, in_specs=in_specs, out_specs=out_specs, check_vma=False)
```

profile of v0, /device:TPU:32, one launch (start us, length us, event | category | flops | bytes accessed | tf_op | source)
XLA Modules:
  0.0 805.6 jit_solution(11040523839631220439)
XLA Ops:
  8.7 96.4 %all-gather.7.cloned.1.call-done = bf16[1024,1024]{1,0:T(8,128)(2,1)} async-done(((bf16[32,1024]{1,0:T(8,128)(2,1)}), bf16[1024,1024]{1,0:T(8,128)(2,1)}) %all-gather.7.cloned.1.call-update) | async-done | bytes 2097168 | tf_op jit(solution)/shard_map/all_gather | solution.py:46
  105.1 4.5 convolution_multiply_fusion.1
  109.7 84.6 %all-gather.9.cloned.1.call-done = bf16[1024,1024]{1,0:T(8,128)(2,1)} async-done(((bf16[32,1024]{1,0:T(8,128)(2,1)}), bf16[1024,1024]{1,0:T(8,128)(2,1)}) %all-gather.9.cloned.1.call-update) | async-done | bytes 2097168 | tf_op jit(solution)/shard_map/all_gather | solution.py:45
  194.3 5.9 multiply_bitcast_fusion.2
  200.2 28.7 %reduce-scatter.5.cloned.1.call-done = f32[128,512]{1,0:T(8,128)} async-done(((f32[1024,512]{1,0:T(8,128)}), f32[128,512]{1,0:T(8,128)}) %reduce-scatter.5.cloned.1.call-update) | async-done | bytes 262160 | tf_op jit(solution)/shard_map/reduce_scatter | solution.py:57
  229.0 56.2 %reduce-scatter.7.cloned.1.call-done = f32[128,1024]{1,0:T(8,128)} async-done(((f32[1024,1024]{1,0:T(8,128)}), f32[128,1024]{1,0:T(8,128)}) %reduce-scatter.7.cloned.1.call-update) | async-done | bytes 524304 | tf_op jit(solution)/shard_map/reduce_scatter | solution.py:14
  285.1 1.9 multiply_convert_fusion.2
  287.1 0.7 pad_maximum_fusion
  289.0 1.3 copy.12
  290.3 37.1 %all-gather.11.cloned.1.call-done = bf16[1024,1024]{1,0:T(8,128)(2,1)} async-done(((bf16[128,1024]{1,0:T(8,128)(2,1)}), bf16[1024,1024]{1,0:T(8,128)(2,1)}) %all-gather.11.cloned.1.call-update) | async-done | bytes 2097168 | tf_op jit(solution)/shard_map/all_gather | solution.py:23
  327.4 4.7 multiply_bitcast_fusion.1
  332.1 0.8 fusion.3
  332.9 91.1 %all-gather.13.cloned.1.call-done = bf16[1024,1024]{1,0:T(8,128)(2,1)} async-done(((bf16[32,1024]{1,0:T(8,128)(2,1)}), bf16[1024,1024]{1,0:T(8,128)(2,1)}) %all-gather.13.cloned.1.call-update) | async-done | bytes 2097168 | tf_op jit(solution)/shard_map/all_gather | solution.py:47
  424.0 5.9 multiply_bitcast_fusion
  430.7 45.1 %reduce-scatter.9.cloned.1.call-done = f32[128,1024]{1,0:T(8,128)} async-done(((f32[1024,1024]{1,0:T(8,128)}), f32[128,1024]{1,0:T(8,128)}) %reduce-scatter.9.cloned.1.call-update) | async-done | bytes 524304 | tf_op jit(solution)/shard_map/reduce_scatter | solution.py:14
  475.8 1.8 fusion.10
  477.6 37.8 %all-gather.17.cloned.1.call-done = bf16[1024,512]{1,0:T(8,128)(2,1)} async-done(((bf16[128,512]{1,0:T(8,128)(2,1)}), bf16[1024,512]{1,0:T(8,128)(2,1)}) %all-gather.17.cloned.1.call-update) | async-done | bytes 1048592 | tf_op jit(solution)/shard_map/all_gather | solution.py:23
  515.4 4.2 add_convert_fusion
  519.5 34.3 %all-gather.15.cloned.1.call-done = bf16[1024,512]{1,0:T(8,128)(2,1)} async-done(((bf16[128,512]{1,0:T(8,128)(2,1)}), bf16[1024,512]{1,0:T(8,128)(2,1)}) %all-gather.15.cloned.1.call-update) | async-done | bytes 1048592 | tf_op jit(solution)/shard_map/all_gather | solution.py:23
  553.8 4.7 convolution_multiply_fusion
  558.6 1.3 copy.14
  559.9 1.3 copy.15
  561.2 236.0 %reduce-scatter.11.cloned.1.call-done = f32[32,1024]{1,0:T(8,128)} async-done(((f32[1024,1024]{1,0:T(8,128)}), f32[32,1024]{1,0:T(8,128)}) %reduce-scatter.11.cloned.1.call-update) | async-done | bytes 131088 | tf_op jit(solution)/shard_map/reduce_scatter | solution.py:85
  797.2 1.5 convert_element_type.36
  (29 shorter events, 3.6 us)
Async XLA Ops:
  7.2 97.9 %all-gather.7.cloned.1.call-start = ((), (), s32[]{:S(2)}) async-start(), calls=%async_computation.4 | async-start | bytes 2162688 | tf_op jit(solution)/shard_map/all_gather | solution.py:46
  7.9 186.4 %all-gather.9.cloned.1.call-start = ((), (), s32[]{:S(2)}) async-start(), calls=%async_computation.6 | async-start | bytes 2162688 | tf_op jit(solution)/shard_map/all_gather | solution.py:45
  8.6 220.3 %reduce-scatter.5.cloned.1.call-start = ((), (), s32[]{:S(2)}) async-start(), calls=%async_computation.5 | async-start | bytes 2359296 | tf_op jit(solution)/shard_map/reduce_scatter | solution.py:57
  109.6 84.7 %copy-start.1 = (bf16[1024,512]{1,0:T(8,128)(2,1)S(1)}, bf16[1024,512]{1,0:T(8,128)(2,1)}, u32[]{:S(2)}) copy-start(bf16[1024,512]{1,0:T(8,128)(2,1)} %param.9) | copy-start | bytes 3145732
  109.6 84.7 %copy-start.2 = (bf16[1024,512]{1,0:T(8,128)(2,1)S(1)}, bf16[1024,512]{1,0:T(8,128)(2,1)}, u32[]{:S(2)}) copy-start(bf16[1024,512]{1,0:T(8,128)(2,1)} %param.10) | copy-start | bytes 3145732
  109.7 175.5 %reduce-scatter.7.cloned.1.call-start = ((), (), s32[]{:S(2)}) async-start(), calls=%async_computation.7 | async-start | bytes 4718592 | tf_op jit(solution)/shard_map/reduce_scatter | solution.py:14
  200.2 127.2 %all-gather.11.cloned.1.call-start = ((), (), s32[]{:S(2)}) async-start(), calls=%async_computation.8 | async-start | bytes 2359296 | tf_op jit(solution)/shard_map/all_gather | solution.py:23
  287.8 136.2 %all-gather.13.cloned.1.call-start = ((), (), s32[]{:S(2)}) async-start(), calls=%async_computation.9 | async-start | bytes 2162688 | tf_op jit(solution)/shard_map/all_gather | solution.py:47
  288.4 187.4 %reduce-scatter.9.cloned.1.call-start = ((), (), s32[]{:S(2)}) async-start(), calls=%async_computation.10 | async-start | bytes 4718592 | tf_op jit(solution)/shard_map/reduce_scatter | solution.py:14
  327.4 4.7 copy-start
  429.9 85.5 %copy-start.3 = (bf16[512,1024]{1,0:T(8,128)(2,1)S(1)}, bf16[512,1024]{1,0:T(8,128)(2,1)}, u32[]{:S(2)}) copy-start(bf16[512,1024]{1,0:T(8,128)(2,1)} %param.11) | copy-start | bytes 3145732
  429.9 85.5 %all-gather.17.cloned.1.call-start = ((), (), s32[]{:S(2)}) async-start(), calls=%async_computation.12 | async-start | bytes 1179648 | tf_op jit(solution)/shard_map/all_gather | solution.py:23
  430.7 123.1 %all-gather.15.cloned.1.call-start = ((), (), s32[]{:S(2)}) async-start(), calls=%async_computation.11 | async-start | bytes 1179648 | tf_op jit(solution)/shard_map/all_gather | solution.py:23
  477.6 319.6 %reduce-scatter.11.cloned.1.call-start = ((), (), s32[]{:S(2)}) async-start(), calls=%async_computation.13 | async-start | bytes 4325376 | tf_op jit(solution)/shard_map/reduce_scatter | solution.py:85
Sparse Core Ops, SparseCore 0:
  11.5 93.5 all-gather.6
  108.6 85.6 all-gather.8
  196.8 32.0 reduce-scatter.4
  231.4 53.7 reduce-scatter.6
  287.9 39.4 all-gather.10
  330.8 93.1 all-gather.12
  430.0 45.6 reduce-scatter.8
  478.1 37.1 all-gather.16
  517.7 36.0 all-gather.14
  558.7 238.4 reduce-scatter.10
where the time goes:
time: 806 us
  waiting for transfers between devices  750 us (93%)
  matrix products  29.9 us (4%)
  between operations  14.2 us (2%)
    reduce_scatter x1, waiting for transfers between devices, body(): lax.psum_scatter(jnp.dot(block_rows, new_down, preferred_element_type=jnp...  236 us
    all_gather x3, waiting for transfers between devices, gather_units(): return lax.all_gather(values, 'mp', axis=0, tiled=True)  109 us
    reduce_scatter x2, waiting for transfers between devices, project_sum(): lax.psum_scatter(jnp.dot(rows_all, weight_pair, preferred_element_type=jn...  101 us
    all_gather x1, waiting for transfers between devices, body(): lax.all_gather(cotangent, 'dp', axis=0, tiled=True)  96.4 us
    all_gather x1, waiting for transfers between devices, body(): lax.all_gather(retain_rows, 'dp', axis=0, tiled=True)  91.1 us
    all_gather x1, waiting for transfers between devices, body(): lax.all_gather(forget_rows, 'dp', axis=0, tiled=True)  84.6 us
    reduce_scatter x1, waiting for transfers between devices, body(): lax.psum_scatter(lax.dot_general(block_rows, w_down, contract_cols, prefe...  28.7 us
  transfers between devices with their start and end apart: 10, of which 10 were waited for; matrix products, arithmetic and copies ran while one was open for 3% of the time, Pallas kernels for 0%

commit v1 on v0

--- a/solution.py
+++ b/solution.py
@@ -7,6 +7,13 @@
 D = 8192
 FF = 16384
 STEP_SIZE = 0.5
+
+
+def refer_copies(v0):
+    shaped = jnp.stack([v0 for _ in range(lax.axis_size("dp"))], axis=0)
+    return jnp.concatenate(
+        lax.all_to_all(shaped, axis_name="dp", split_axis=0, concat_axis=0), axis=0
+    )
 
 
 def project_sum(rows_all, weight_pair):
@@ -43,7 +50,7 @@
     contract_cols = (((1,), (1,)), ((), ()))
     forget_all, cotan_all, retain_all = (
         lax.all_gather(forget_rows, "dp", axis=0, tiled=True),
-        lax.all_gather(cotangent, "dp", axis=0, tiled=True),
+        refer_copies(cotangent),
         lax.all_gather(retain_rows, "dp", axis=0, tiled=True),
     )
     total_rows = forget_all.shape[0]

time: 806 us -> 708 us (0.88)
  waiting for transfers between devices: 750 us -> 636 us
  starting transfers between devices: 0.4 us -> 13.7 us
    all_gather x1 -> x0, waiting for transfers between devices: 96.4 us -> none  [body(): lax.all_gather(cotangent, 'dp', axis=0, tiled=True)]
    all_to_all x0 -> x1, waiting for transfers between devices: none -> 55.9 us  [refer_copies(): lax.all_to_all(shaped, axis_name='dp', split_axis=0, concat_axis=0)]
    all_gather x1, waiting for transfers between devices: 84.6 us -> 47 us  [body(): lax.all_gather(forget_rows, 'dp', axis=0, tiled=True)]
    reduce_scatter x1, waiting for transfers between devices: 28.7 us -> 0.02 us  [body(): lax.psum_scatter(lax.dot_general(block_rows, w_down, contract_cols, prefe...]
    all_to_all x0 -> x1, starting transfers between devices: none -> 13.2 us  [refer_copies(): lax.all_to_all(shaped, axis_name='dp', split_axis=0, concat_axis=0)]
  transfers between devices with their start and end apart: 10 -> 10, of which waited for: 10 -> 9; matrix products, arithmetic and copies ran while one was open for 3% -> 3% of each run, Pallas kernels for 0% -> 0%
where the time goes in v1:
time: 708 us; the launch traced here: 707 us
  waiting for transfers between devices  636 us (90%)
  matrix products  28 us (4%)
  between operations  15.6 us (2%)
  starting transfers between devices  13.7 us (2%)
    reduce_scatter x1, waiting for transfers between devices, body(): lax.psum_scatter(jnp.dot(block_rows, new_down, preferred_element_type=jnp...  235 us
    all_gather x3, waiting for transfers between devices, gather_units(): return lax.all_gather(values, 'mp', axis=0, tiled=True)  108 us
    reduce_scatter x2, waiting for transfers between devices, project_sum(): lax.psum_scatter(jnp.dot(rows_all, weight_pair, preferred_element_type=jn...  96.1 us
    all_gather x1, waiting for transfers between devices, body(): lax.all_gather(retain_rows, 'dp', axis=0, tiled=True)  91.6 us
    all_to_all x1, waiting for transfers between devices, refer_copies(): lax.all_to_all(shaped, axis_name='dp', split_axis=0, concat_axis=0)  55.9 us
    all_gather x1, waiting for transfers between devices, body(): lax.all_gather(forget_rows, 'dp', axis=0, tiled=True)  47 us
  transfers between devices with their start and end apart: 10, of which 9 were waited for; matrix products, arithmetic and copies ran while one was open for 3% of the time, Pallas kernels for 0%

profile of v1, /device:TPU:32, one launch (start us, length us, event | category | flops | bytes accessed | tf_op | source)
XLA Modules:
  0.0 707.1 jit_solution(4626845556636008805)
XLA Ops:
  8.0 2.4 stack.2
  10.4 13.2 %all-to-all-start = ((bf16[32,32,1024]{2,1,0:T(8,128)(2,1)}), bf16[32,32,1024]{2,1,0:T(8,128)(2,1)S(1)}, u32[]{:S(2)}, u32[]{:S(2)}) async-start(bf16[32,32,1024]{2,1,0:T(8,128)(2,1)} %stack.2), calls=%async_computation | async-start | bytes 4194304 | tf_op jit(solution)/shard_map/all_to_all | solution.py:15
  24.4 55.9 %all-to-all-done = bf16[32,32,1024]{2,1,0:T(8,128)(2,1)S(1)} async-done(((bf16[32,32,1024]{2,1,0:T(8,128)(2,1)}), bf16[32,32,1024]{2,1,0:T(8,128)(2,1)S(1)}, u32[]{:S(2)}, u32[]{:S(2)}) %all-to-all-start) | async-done | bytes 2097184 | tf_op jit(solution)/shard_map/all_to_all | solution.py:15
  80.3 2.7 convolution_multiply_fusion.1
  83.1 47.0 %all-gather.6.cloned.1.call-done = bf16[1024,1024]{1,0:T(8,128)(2,1)} async-done(((bf16[32,1024]{1,0:T(8,128)(2,1)}), bf16[1024,1024]{1,0:T(8,128)(2,1)}) %all-gather.6.cloned.1.call-update) | async-done | bytes 2097168 | tf_op jit(solution)/shard_map/all_gather | solution.py:52
  130.1 5.9 multiply_bitcast_fusion.2
  136.1 51.0 %reduce-scatter.7.cloned.1.call-done = f32[128,1024]{1,0:T(8,128)} async-done(((f32[1024,1024]{1,0:T(8,128)}), f32[128,1024]{1,0:T(8,128)}) %reduce-scatter.7.cloned.1.call-update) | async-done | bytes 524304 | tf_op jit(solution)/shard_map/reduce_scatter | solution.py:21
  187.1 1.9 multiply_convert_fusion.2
  191.1 1.3 copy.12
  192.4 36.6 %all-gather.8.cloned.1.call-done = bf16[1024,1024]{1,0:T(8,128)(2,1)} async-done(((bf16[128,1024]{1,0:T(8,128)(2,1)}), bf16[1024,1024]{1,0:T(8,128)(2,1)}) %all-gather.8.cloned.1.call-update) | async-done | bytes 2097168 | tf_op jit(solution)/shard_map/all_gather | solution.py:30
  229.0 4.7 multiply_bitcast_fusion.1
  233.8 0.8 fusion.3
  234.5 91.6 %all-gather.10.cloned.1.call-done = bf16[1024,1024]{1,0:T(8,128)(2,1)} async-done(((bf16[32,1024]{1,0:T(8,128)(2,1)}), bf16[1024,1024]{1,0:T(8,128)(2,1)}) %all-gather.10.cloned.1.call-update) | async-done | bytes 2097168 | tf_op jit(solution)/shard_map/all_gather | solution.py:54
  326.1 5.9 multiply_bitcast_fusion
  332.8 45.1 %reduce-scatter.9.cloned.1.call-done = f32[128,1024]{1,0:T(8,128)} async-done(((f32[1024,1024]{1,0:T(8,128)}), f32[128,1024]{1,0:T(8,128)}) %reduce-scatter.9.cloned.1.call-update) | async-done | bytes 524304 | tf_op jit(solution)/shard_map/reduce_scatter | solution.py:21
  377.9 1.8 fusion.10
  379.9 37.4 %all-gather.14.cloned.1.call-done = bf16[1024,512]{1,0:T(8,128)(2,1)} async-done(((bf16[128,512]{1,0:T(8,128)(2,1)}), bf16[1024,512]{1,0:T(8,128)(2,1)}) %all-gather.14.cloned.1.call-update) | async-done | bytes 1048592 | tf_op jit(solution)/shard_map/all_gather | solution.py:30
  417.3 4.2 add_convert_fusion
  421.4 34.1 %all-gather.12.cloned.1.call-done = bf16[1024,512]{1,0:T(8,128)(2,1)} async-done(((bf16[128,512]{1,0:T(8,128)(2,1)}), bf16[1024,512]{1,0:T(8,128)(2,1)}) %all-gather.12.cloned.1.call-update) | async-done | bytes 1048592 | tf_op jit(solution)/shard_map/all_gather | solution.py:30
  455.5 4.7 convolution_multiply_fusion
  460.2 1.3 copy.14
  461.6 1.3 copy.15
  462.9 235.3 %reduce-scatter.11.cloned.1.call-done = f32[32,1024]{1,0:T(8,128)} async-done(((f32[1024,1024]{1,0:T(8,128)}), f32[32,1024]{1,0:T(8,128)}) %reduce-scatter.11.cloned.1.call-update) | async-done | bytes 131088 | tf_op jit(solution)/shard_map/reduce_scatter | solution.py:92
  698.1 1.5 convert_element_type.36
  (35 shorter events, 4.0 us)
Async XLA Ops:
  10.4 69.9 %copy-start.5 = (bf16[512,1024]{1,0:T(8,128)(2,1)S(1)}, bf16[512,1024]{1,0:T(8,128)(2,1)}, u32[]{:S(2)}) copy-start(bf16[512,1024]{1,0:T(8,128)(2,1)} %param.11) | copy-start | bytes 3145732
  10.4 69.9 %all-to-all-start = ((bf16[32,32,1024]{2,1,0:T(8,128)(2,1)}), bf16[32,32,1024]{2,1,0:T(8,128)(2,1)S(1)}, u32[]{:S(2)}, u32[]{:S(2)}) async-start(bf16[32,32,1024]{2,1,0:T(8,128)(2,1)} %stack.2), calls=%async_computation | async-start | bytes 4194304 | tf_op jit(solution)/shard_map/all_to_all | solution.py:15
  23.6 106.5 %all-gather.6.cloned.1.call-start = ((), (), s32[]{:S(2)}) async-start(), calls=%async_computation.6 | async-start | bytes 2162688 | tf_op jit(solution)/shard_map/all_gather | solution.py:52
  24.4 111.7 %reduce-scatter.5.cloned.1.call-start = ((), (), s32[]{:S(2)}) async-start(), calls=%async_computation.5 | async-start | bytes 2359296 | tf_op jit(solution)/shard_map/reduce_scatter | solution.py:64
  80.3 2.7 copy-start.1
  83.0 47.1 %copy-start.2 = (bf16[1024,512]{1,0:T(8,128)(2,1)S(1)}, bf16[1024,512]{1,0:T(8,128)(2,1)}, u32[]{:S(2)}) copy-start(bf16[1024,512]{1,0:T(8,128)(2,1)} %param.9) | copy-start | bytes 3145732
  83.0 47.1 %copy-start.4 = (bf16[1024,512]{1,0:T(8,128)(2,1)S(1)}, bf16[1024,512]{1,0:T(8,128)(2,1)}, u32[]{:S(2)}) copy-start(bf16[1024,512]{1,0:T(8,128)(2,1)} %param.10) | copy-start | bytes 3145732
  83.1 104.0 %reduce-scatter.7.cloned.1.call-start = ((), (), s32[]{:S(2)}) async-start(), calls=%async_computation.7 | async-start | bytes 4718592 | tf_op jit(solution)/shard_map/reduce_scatter | solution.py:21
  136.0 54.6 %copy-start.3 = (bf16[1024,512]{1,0:T(8,128)(2,1)S(1)}, bf16[1024,512]{1,0:T(8,128)(2,1)}, u32[]{:S(2)}) copy-start(bf16[1024,512]{1,0:T(8,128)(2,1)} %param.9) | copy-start | bytes 3145732
  136.0 93.0 %all-gather.8.cloned.1.call-start = ((), (), s32[]{:S(2)}) async-start(), calls=%async_computation.8 | async-start | bytes 2359296 | tf_op jit(solution)/shard_map/all_gather | solution.py:30
  189.8 136.3 %all-gather.10.cloned.1.call-start = ((), (), s32[]{:S(2)}) async-start(), calls=%async_computation.9 | async-start | bytes 2162688 | tf_op jit(solution)/shard_map/all_gather | solution.py:54
  190.5 187.4 %reduce-scatter.9.cloned.1.call-start = ((), (), s32[]{:S(2)}) async-start(), calls=%async_computation.10 | async-start | bytes 4718592 | tf_op jit(solution)/shard_map/reduce_scatter | solution.py:21
  229.0 4.7 copy-start
  332.0 85.3 %copy-start.6 = (bf16[512,1024]{1,0:T(8,128)(2,1)S(1)}, bf16[512,1024]{1,0:T(8,128)(2,1)}, u32[]{:S(2)}) copy-start(bf16[512,1024]{1,0:T(8,128)(2,1)} %param.11) | copy-start | bytes 3145732
  332.0 85.2 %all-gather.14.cloned.1.call-start = ((), (), s32[]{:S(2)}) async-start(), calls=%async_computation.12 | async-start | bytes 1179648 | tf_op jit(solution)/shard_map/all_gather | solution.py:30
  332.8 122.7 %all-gather.12.cloned.1.call-start = ((), (), s32[]{:S(2)}) async-start(), calls=%async_computation.11 | async-start | bytes 1179648 | tf_op jit(solution)/shard_map/all_gather | solution.py:30
  379.7 318.5 %reduce-scatter.11.cloned.1.call-start = ((), (), s32[]{:S(2)}) async-start(), calls=%async_computation.13 | async-start | bytes 4325376 | tf_op jit(solution)/shard_map/reduce_scatter | solution.py:92
Sparse Core Ops, SparseCore 0:
  28.0 102.1 all-gather.5
  460.4 237.7 reduce-scatter.10
Sparse Core Ops, SparseCore 1:
  83.1 45.4 reduce-scatter.4
  136.1 50.9 reduce-scatter.6
  189.9 39.1 all-gather.7
  232.6 93.4 all-gather.9
  332.1 45.7 reduce-scatter.8
  380.3 36.9 all-gather.13
  419.5 35.9 all-gather.11
